TPU v7x, 512 devices: a whole 4x4x16 slice. The times are simulated.
512 devices in a mesh: ctx: 16 (over z), ep: 32 (over y, x, core).
Axes of the slice: x: 4, y: 4, z: 16, core: 2. Of those that a mesh axis runs over, the one named last changes fastest.
Arguments:
- query_act: bfloat16 [2048, 8192], P('ctx', 'ep'), may hold values from -6 to 6
- key_act: bfloat16 [2048, 8192], P('ctx', 'ep'), may hold values from -6 to 6
- value_act: bfloat16 [2048, 8192], P('ctx', 'ep'), may hold values from -6 to 6
- state_init: float32 [64, 128, 128], P('ep'), may hold values from -128 to 128
- head_gain: float32 [8192], P('ep'), may hold values from 0.25 to 1.75
- out_weight: bfloat16 [8192, 3072], P('ctx', 'ep'), may hold values from -0.0625 to 0.0625
- stream_in: bfloat16 [2048, 3072], P('ctx', 'ep'), may hold values from -150 to 150
- model_gain: float32 [3072], replicated, may hold values from 0.25 to 1.75
- expert_ids: int32 [2048, 2], P('ctx'), may hold values from 0 to 15, as said below
- expert_slots: int32 [2048, 2], P('ctx'), may hold values from 0 to 19, as said below
- route_gates: float32 [2048, 2], P('ctx'), may hold values from 0.2 to 1
- gate_weight: bfloat16 [32, 3072, 3072], P('ep', 'ctx'), may hold values from -0.109375 to 0.109375
- up_weight: bfloat16 [32, 3072, 3072], P('ep', 'ctx'), may hold values from -0.109375 to 0.109375
- down_weight: bfloat16 [32, 3072, 3072], P('ep', 'ctx'), may hold values from -0.078125 to 0.078125
- out_grad: bfloat16 [2048, 3072], P('ctx', 'ep'), may hold values from -6 to 6
Outputs:
- layer_out: bfloat16 [2048, 3072], P('ctx', 'ep')
- grad_query: bfloat16 [2048, 8192], P('ctx', 'ep')
- grad_key: bfloat16 [2048, 8192], P('ctx', 'ep')
- grad_value: bfloat16 [2048, 8192], P('ctx', 'ep')
- grad_state: float32 [64, 128, 128], P('ep')
- grad_stream: bfloat16 [2048, 3072], P('ctx', 'ep')
Inputs may be any that keep to these rules, and one draw needn't show every extreme that they name: `expert_ids`: within each block of 128 tokens a token's two experts differ; the tokens naming expert e hold the slots 0 to n - 1 of e once each, n being their number; no expert is named by more than 20 tokens of a block, and in every block some expert by exactly 20. `expert_slots`: see expert_ids.
All inputs are finite; a program needn't handle non-finite values.
Results may differ from a plain program's by a relative error of at most 0.02.
Values may be sent and summed in bfloat16 or wider, within the bound.
No kernel may reach another device: no remote copies, remote signals or barrier semaphores. Data moves between devices by JAX's collectives and lax.ppermute only.
A program may use at most 64 MiB of HBM per device.

v0:
```python
import jax
import jax.numpy as jnp
from jax import lax
from jax.sharding import PartitionSpec as P


def carried_in(value, axis, join, neutral, backward):
    count = lax.axis_size(axis)
    place = lax.axis_index(axis)
    ahead = count - 1 - place if backward else place
    gathered = lax.all_gather(value.astype(jnp.bfloat16), axis)
    state = jnp.zeros_like(value) + jnp.asarray(neutral, value.dtype)

    def one(turn, state):
        source = count - 1 - turn if backward else turn
        return join(state, lax.dynamic_index_in_dim(gathered, source, 0, False).astype(value.dtype))

    return lax.fori_loop(0, ahead, one, state)


def head_normalize(attended, gain):
    factor = lax.rsqrt(jnp.mean(attended * attended, -1, keepdims=True) + 1e-06)
    return attended * factor * gain


def add_states(earlier, later_one):
    return earlier + later_one


def contract_last(left, right):
    return lax.dot_general(
        left, right, (((1,), (1,)), ((), ())), preferred_element_type=jnp.float32
    )


def local(
    query_act,
    key_act,
    value_act,
    state_init,
    head_gain,
    out_weight,
    stream_in,
    model_gain,
    expert_ids,
    expert_slots,
    route_gates,
    gate_weight,
    up_weight,
    down_weight,
    out_grad,
):
    f32 = jnp.float32
    high = lax.Precision.HIGHEST
    ep_count = lax.axis_size("ep")
    expert_count = ep_count // 2
    my_ep = lax.axis_index("ep")
    tokens_here = query_act.shape[0]
    head_count = state_init.shape[0]
    head_size = state_init.shape[1]
    model_width = model_gain.shape[0]
    columns = stream_in.shape[1]
    capacity = 5 * tokens_here // (2 * expert_count)
    query3 = query_act.reshape(tokens_here, head_count, head_size)
    key3 = key_act.reshape(tokens_here, head_count, head_size)
    value3 = value_act.reshape(tokens_here, head_count, head_size)
    kv_own = jnp.einsum("thd,the->hde", key3, value3, preferred_element_type=f32)
    zero_state = jnp.zeros_like(kv_own)
    before = carried_in(kv_own, "ctx", add_states, zero_state, False)
    prefix = state_init + before
    causal = jnp.arange(tokens_here)[:, None] >= jnp.arange(tokens_here)[None, :]
    scores = jnp.einsum("thd,shd->hts", query3, key3, preferred_element_type=f32)
    scores_bf = jnp.where(causal[None], scores, 0.0).astype(jnp.bfloat16)
    inside = jnp.einsum("hts,she->the", scores_bf, value3, preferred_element_type=f32)
    from_state = jnp.einsum("thd,hde->the", query3.astype(f32), prefix, precision=high)
    attended = from_state + inside
    gain_heads = head_gain.reshape(head_count, head_size)
    normed_heads = (
        head_normalize(attended, gain_heads)
        .astype(jnp.bfloat16)
        .reshape(tokens_here, head_count * head_size)
    )
    w_cols = lax.all_gather(out_weight, "ctx", axis=0, tiled=True)
    attn_proj = jnp.dot(
        lax.all_gather(normed_heads, "ep", axis=1, tiled=True), w_cols, preferred_element_type=f32
    )
    stream = (stream_in.astype(f32) + attn_proj).astype(jnp.bfloat16)
    stream_f = stream.astype(f32)
    gain_cols = lax.dynamic_slice_in_dim(model_gain, my_ep * columns, columns, 0)
    dest_expert = jnp.arange(ep_count) % expert_count
    slot_iota = jnp.arange(capacity)
    hits = (expert_ids[:, :, None, None] == dest_expert[None, None, :, None]) & (
        expert_slots[:, :, None, None] == slot_iota[None, None, None, :]
    )
    hits_f = hits.astype(f32)
    dest_picks = jnp.sum(hits_f, 1).reshape(tokens_here, ep_count * capacity)
    dest_weights = jnp.sum(hits_f * route_gates[:, :, None, None], 1).reshape(
        tokens_here, ep_count * capacity
    )
    whole_rows = lax.all_gather(stream, "ep", axis=1, tiled=True).astype(f32)
    row_scale = lax.rsqrt(jnp.mean(whole_rows * whole_rows, -1, keepdims=True) + 1e-05)
    model_in = (whole_rows * row_scale * model_gain).astype(jnp.bfloat16)
    own_select = lax.dynamic_slice_in_dim(dest_picks, my_ep * capacity, capacity, 1).T.astype(
        jnp.bfloat16
    )
    expert_in = jnp.dot(own_select, model_in, preferred_element_type=f32).astype(jnp.bfloat16)
    w_gate = gate_weight[0]
    w_up = up_weight[0]
    w_down = down_weight[0]
    hidden_block = w_gate.shape[0]
    portion = lax.all_gather(expert_in, "ctx", axis=0, tiled=True)
    projected = jnp.concatenate([contract_last(portion, w_gate), contract_last(portion, w_up)], 1)
    pre_gate = projected[:, :hidden_block]
    pre_up = projected[:, hidden_block:]
    gate_sig = jax.nn.sigmoid(pre_gate)
    activated = (pre_gate * gate_sig * pre_up).astype(jnp.bfloat16)
    half_out = lax.psum_scatter(
        jnp.dot(activated, w_down, preferred_element_type=f32).astype(jnp.bfloat16),
        "ctx",
        scatter_dimension=0,
        tiled=True,
    )
    returned = lax.all_to_all(half_out, "ep", split_axis=1, concat_axis=0, tiled=True)
    expert_mix = jnp.dot(dest_weights, returned.astype(f32), precision=high)
    layer_out = (stream_f + expert_mix).astype(jnp.bfloat16)
    grad_out = out_grad.astype(f32)
    grad_send = jnp.dot(dest_weights.T, grad_out, precision=high).astype(jnp.bfloat16)
    grad_in = lax.all_to_all(grad_send, "ep", split_axis=0, concat_axis=1, tiled=True)
    grad_act = contract_last(lax.all_gather(grad_in, "ctx", axis=0, tiled=True), w_down)
    grad_gate_pre = (grad_act * pre_up * gate_sig * (1.0 + pre_gate * (1.0 - gate_sig))).astype(
        jnp.bfloat16
    )
    grad_up_pre = (grad_act * pre_gate * gate_sig).astype(jnp.bfloat16)
    grad_half = lax.psum_scatter(
        (
            jnp.dot(grad_gate_pre, w_gate, preferred_element_type=f32)
            + jnp.dot(grad_up_pre, w_up, preferred_element_type=f32)
        ).astype(jnp.bfloat16),
        "ctx",
        scatter_dimension=0,
        tiled=True,
    )
    grad_back = lax.all_to_all(grad_half, "ep", split_axis=1, concat_axis=0, tiled=True)
    grad_model_in = jnp.dot(dest_picks, grad_back.astype(f32), precision=high)
    scaled_grad = grad_model_in * gain_cols
    inner_sum = lax.psum(jnp.sum(stream_f * scaled_grad, -1), "ep")
    grad_stream = (
        grad_out
        + row_scale * scaled_grad
        - stream_f * row_scale**3 * inner_sum[:, None] / model_width
    ).astype(jnp.bfloat16)
    w_rows = lax.all_to_all(w_cols, "ep", split_axis=0, concat_axis=1, tiled=True)
    grad_heads = contract_last(lax.all_gather(grad_stream, "ep", axis=1, tiled=True), w_rows)
    head_pull = jax.vjp(lambda value: head_normalize(value, gain_heads), attended)[1]
    grad_attended = head_pull(grad_heads.reshape(tokens_here, head_count, head_size))[0].astype(
        jnp.bfloat16
    )
    state_part = jnp.einsum("thd,the->hde", query3, grad_attended, preferred_element_type=f32)
    later_sum = carried_in(state_part, "ctx", add_states, zero_state, True)
    state_total = lax.psum(state_part.astype(jnp.bfloat16), "ctx").astype(jnp.float32)
    grad_scores = jnp.einsum("the,she->hts", grad_attended, value3, preferred_element_type=f32)
    grad_masked = jnp.where(causal[None], grad_scores, 0.0).astype(jnp.bfloat16)
    grad_att_f = grad_attended.astype(f32)
    grad_query = jnp.einsum("the,hde->thd", grad_att_f, prefix, precision=high) + jnp.einsum(
        "hts,shd->thd", grad_masked, key3, preferred_element_type=f32
    )
    grad_key = jnp.einsum(
        "the,hde->thd", value3.astype(f32), later_sum, precision=high
    ) + jnp.einsum("hts,thd->shd", grad_masked, query3, preferred_element_type=f32)
    grad_value = jnp.einsum(
        "thd,hde->the", key3.astype(f32), later_sum, precision=high
    ) + jnp.einsum("hts,the->she", scores_bf, grad_attended, preferred_element_type=f32)
    flat_shape = (tokens_here, head_count * head_size)
    return (
        layer_out,
        grad_query.astype(jnp.bfloat16).reshape(flat_shape),
        grad_key.astype(jnp.bfloat16).reshape(flat_shape),
        grad_value.astype(jnp.bfloat16).reshape(flat_shape),
        state_total,
        grad_stream,
    )


def solution(mesh):
    return jax.shard_map(
        local,
        mesh=mesh,
        in_specs=(
            P("ctx", "ep"),
            P("ctx", "ep"),
            P("ctx", "ep"),
            P("ep", None, None),
            P("ep"),
            P("ctx", "ep"),
            P("ctx", "ep"),
            P(),
            P("ctx", None),
            P("ctx", None),
            P("ctx", None),
            P("ep", "ctx", None),
            P("ep", "ctx", None),
            P("ep", "ctx", None),
            P("ctx", "ep"),
        ),
        out_specs=(
            P("ctx", "ep"),
            P("ctx", "ep"),
            P("ctx", "ep"),
            P("ctx", "ep"),
            P("ep", None, None),
            P("ctx", "ep"),
        ),
        check_vma=False,
    )
```

profile of v0, /device:TPU:2, one launch (start us, length us, event | category | flops | bytes accessed | tf_op | source)
XLA Modules:
  0.0 797.9 jit_solution(11163868636489932232)
XLA Ops:
  12.9 72.9 %all-gather.15.cloned.1.call-done = bf16[32,128,128]{2,1,0:T(8,128)(2,1)} async-done(((bf16[2,128,128]{2,1,0:T(8,128)(2,1)}), bf16[32,128,128]{2,1,0:T(8,128)(2,1)}) %all-gather.15.cloned.1.call-update) | async-done | bytes 1048592 | tf_op jit(solution)/shard_map/all_gather | solution.py:11
  88.5 14.3 %all_to_all.67 = bf16[32,20,96]{2,1,0:T(8,128)(2,1)S(1)} all-to-all(bf16[32,20,96]{2,1,0:T(8,128)(2,1)S(1)} %all_to_all.53), channel_id=1, replica_groups=mesh['ctx'=16,'ep'=32] {'ep'}, dimensions={0} | all-to-all | bytes 245760 | tf_op jit(solution)/shard_map/all_to_all | solution.py:128
  104.0 52.8 %all-gather.13.cloned.1.call-done = bf16[8192,96]{0,1:T(8,128)(2,1)} async-done(((bf16[512,96]{0,1:T(8,128)(2,1)}), bf16[8192,96]{0,1:T(8,128)(2,1)}) %all-gather.13.cloned.1.call-update) | async-done | bytes 1572880 | tf_op jit(solution)/shard_map/all_gather | solution.py:83
  156.8 59.4 %all-gather.11.cloned.1.call-done = bf16[128,8192]{0,1:T(8,128)(2,1)} async-done(((bf16[128,256]{0,1:T(8,128)(2,1)}), bf16[128,8192]{0,1:T(8,128)(2,1)}) %all-gather.11.cloned.1.call-update) | async-done | bytes 2097168 | tf_op jit(solution)/shard_map/all_gather | solution.py:85
  216.3 2.6 fusion.33
  219.5 23.3 %all_gather.34 = bf16[128,3072]{0,1:T(8,128)(2,1)S(1)} all-gather(bf16[128,96]{0,1:T(8,128)(2,1)S(1)} %fusion.33), channel_id=1, replica_groups=mesh['ctx'=16,'ep'=32] {'ep'}, dimensions={1}, use_global_device_ids=true | all-gather | bytes 811008 | tf_op jit(solution)/shard_map/all_gather | solution.py:100
  246.5 6.2 all-to-all-start.3
  252.7 38.8 %all-gather.21.cloned.1.call-done = bf16[16,20,3072]{2,1,0:T(8,128)(2,1)} async-done(((bf16[1,20,3072]{2,1,0:T(8,128)(2,1)}), bf16[16,20,3072]{2,1,0:T(8,128)(2,1)}) %all-gather.21.cloned.1.call-update) | async-done | bytes 1966096 | tf_op jit(solution)/shard_map/all_gather | solution.py:129
  295.7 67.7 %all-gather.19.cloned.1.call-done = bf16[16,20,3072]{2,1,0:T(8,128)(2,1)} async-done(((bf16[1,20,3072]{2,1,0:T(8,128)(2,1)}), bf16[16,20,3072]{2,1,0:T(8,128)(2,1)}) %all-gather.19.cloned.1.call-update) | async-done | bytes 1966096 | tf_op jit(solution)/shard_map/all_gather | solution.py:111
  373.4 52.9 %fusion.70 = (bf16[24,3072]{1,0:T(8,128)(2,1)}, bf16[24,3072]{1,0:T(8,128)(2,1)}) fusion(bf16[320,3072]{1,0:T(8,128)(2,1)S(1)} %convolution_convert_fusion, bf16[320,3072]{1,0:T(8,128)(2,1)} %fusion.2), kind=kCustom, calls=%all-reduce-scatter.2 | all-reduce-scatter fusion | flops 2359297 | bytes 4229120
  427.3 5.2 collective-permute-start
  432.5 6.7 collective-permute-start.1
  440.9 4.2 collective-permute-start.3
  445.1 5.4 collective-permute-start.4
  451.5 5.0 collective-permute-start.5
  463.6 7.5 all-to-all-start.2
  474.1 4.1 all-to-all-done.2
  480.7 60.3 %psum.14 = f32[128]{0:T(128)S(1)} all-reduce(f32[128]{0:T(128)} %get-tuple-element.145), channel_id=1, replica_groups=mesh['ctx'=16,'ep'=32] {'ep'}, use_global_device_ids=true, to_apply=%region_9.10 | all-reduce | flops 128 | bytes 1024 | tf_op jit(solution)/shard_map/psum | solution.py:146
  542.5 27.4 %all_gather.37 = bf16[128,3072]{0,1:T(8,128)(2,1)S(1)} all-gather(bf16[128,96]{0,1:T(8,128)(2,1)S(1)} %fusion.59), channel_id=1, replica_groups=mesh['ctx'=16,'ep'=32] {'ep'}, dimensions={1}, use_global_device_ids=true | all-gather | bytes 811008 | tf_op jit(solution)/shard_map/all_gather | solution.py:153
  575.5 5.6 all-to-all-start
  582.5 5.7 all-to-all-done
  589.1 117.0 %all-reduce.7.cloned.1.call-done = bf16[2,128,128]{1,2,0:T(8,128)(2,1)} async-done(((bf16[2,128,128]{1,2,0:T(8,128)(2,1)}), bf16[2,128,128]{1,2,0:T(8,128)(2,1)}) %all-reduce.7.cloned.1.call-update) | async-done | bytes 65552 | tf_op jit(solution)/shard_map/psum | solution.py:160
  707.7 67.6 %all-gather.17.cloned.1.call-done = bf16[32,128,128]{2,1,0:T(8,128)(2,1)} async-done(((bf16[2,128,128]{2,1,0:T(8,128)(2,1)}), bf16[32,128,128]{2,1,0:T(8,128)(2,1)}) %all-gather.17.cloned.1.call-update) | async-done | bytes 1048592 | tf_op jit(solution)/shard_map/all_gather | solution.py:11
  775.3 13.4 %while.23 = (s32[]{:T(128)}, f32[2,128,128]{2,1,0:T(8,128)S(1)}, s32[]{:T(128)}, bf16[16,2,128,128]{3,2,1,0:T(8,128)(2,1)}, s32[]{:T(128)}, /*index=5*/s32[]{:T(128)}, s32[]{:T(128)}, s32[]{:T(128)}) while((s32[]{:T(128)}, f32[2,128,128]{2,1,0:T(8,128)S(1)}, s32[]{:T(128)}, bf16[16,2,128,128]{3,2,1,0:T(8,128)(2,1)}, s32[]{:T(128)}, ...), condition=%wide.region_12.13_spmd, body=%wide.region_11.12_spmd.sunk | while | flops 65542 | bytes 327815 | solution.py:18
  (182 shorter events, 69.3 us)
Async XLA Ops:
  7.2 286.8 %copy-start = (bf16[1,192,3072]{2,1,0:T(8,128)(2,1)S(1)}, bf16[1,192,3072]{2,1,0:T(8,128)(2,1)}, u32[]{:S(2)}) copy-start(bf16[1,192,3072]{2,1,0:T(8,128)(2,1)} %param.32) | copy-start | bytes 3538948
  7.2 78.7 %copy-start.24 = (f32[2,128,128]{2,1,0:T(8,128)S(1)}, f32[2,128,128]{2,1,0:T(8,128)}, u32[]{:S(2)}) copy-start(f32[2,128,128]{2,1,0:T(8,128)} %param.22) | copy-start | bytes 393220
  7.2 78.6 %all-gather.15.cloned.1.call-start = ((), (), s32[]{:S(2)}) async-start(), calls=%async_computation.7 | async-start | bytes 1114112 | tf_op jit(solution)/shard_map/all_gather | solution.py:11
  8.3 77.5 %copy-start.16 = (bf16[128,256]{0,1:T(8,128)(2,1)}, bf16[128,256]{0,1:T(8,128)(2,1)S(1)}, u32[]{:S(2)}) copy-start(bf16[128,256]{0,1:T(8,128)(2,1)S(1)} %copy.182) | copy-start | bytes 196612
  10.0 76.3 %copy-start.18 = (bf16[128,256]{1,0:T(8,128)(2,1)S(1)}, bf16[128,256]{1,0:T(8,128)(2,1)}, u32[]{:S(2)}) copy-start(bf16[128,256]{1,0:T(8,128)(2,1)} %param.21) | copy-start | bytes 196612
  10.0 146.8 %all-gather.13.cloned.1.call-start = ((), (), s32[]{:S(2)}) async-start(), calls=%async_computation.5 | async-start | bytes 1671168 | tf_op jit(solution)/shard_map/all_gather | solution.py:83
  10.7 205.5 %all-gather.11.cloned.1.call-start = ((), (), s32[]{:S(2)}) async-start(), calls=%async_computation.4 | async-start | bytes 2162688 | tf_op jit(solution)/shard_map/all_gather | solution.py:85
  87.3 204.1 %all-gather.21.cloned.1.call-start = ((), (), s32[]{:S(2)}) async-start(), calls=%async_computation.10 | async-start | bytes 2506752 | tf_op jit(solution)/shard_map/all_gather | solution.py:129
  87.9 128.3 %copy-start.27 = (bf16[128,96]{0,1:T(8,128)(2,1)S(1)}, bf16[128,96]{0,1:T(8,128)(2,1)}, u32[]{:S(2)}) copy-start(bf16[128,96]{0,1:T(8,128)(2,1)} %param.25) | copy-start | bytes 73732
  103.7 259.7 %all-gather.19.cloned.1.call-start = ((), (), s32[]{:S(2)}) async-start(), calls=%async_computation.9 | async-start | bytes 2506752 | tf_op jit(solution)/shard_map/all_gather | solution.py:111
  246.5 217.2 %all-to-all-start.3 = ((bf16[32,256,96]{1,2,0:T(8,128)(2,1)}), bf16[32,256,96]{1,2,0:T(8,128)(2,1)}, u32[]{:S(2)}, u32[]{:S(2)}) async-start(bf16[32,256,96]{1,2,0:T(8,128)(2,1)} %bitcast.161), calls=%async_computation.3 | async-start | bytes 3145728 | tf_op jit(solution)/shard_map/all_to_all | solution.py:152
  427.3 31.1 %collective-permute-start = (bf16[24,3072]{1,0:T(8,128)(2,1)}, bf16[24,3072]{1,0:T(8,128)(2,1)S(1)}, u32[]{:S(2)}, u32[]{:S(2)}) collective-permute-start(bf16[24,3072]{1,0:T(8,128)(2,1)} %get-tuple-element.139), channel_id=1, source_target_pairs={{0,32},{32,64},{64,96},{96,128},{128,160},{160,192},{192,224},{224... | collective-permute-start | bytes 442376
  432.5 25.9 %collective-permute-start.1 = (bf16[24,3072]{1,0:T(8,128)(2,1)}, bf16[24,3072]{1,0:T(8,128)(2,1)S(1)}, u32[]{:S(2)}, u32[]{:S(2)}) collective-permute-start(bf16[24,3072]{1,0:T(8,128)(2,1)} %get-tuple-element.139), channel_id=1, source_target_pairs={{0,64},{32,96},{64,128},{96,160},{128,192},{160,224},{192,256},{22... | collective-permute-start | bytes 442376
  439.3 12.2 %collective-permute-start.2 = (bf16[12,3072]{1,0:T(8,128)(2,1)S(1)}, bf16[12,3072]{1,0:T(8,128)(2,1)S(1)}, u32[]{:S(2)}, u32[]{:S(2)}) collective-permute-start(bf16[12,3072]{1,0:T(8,128)(2,1)S(1)} %slice), channel_id=1, source_target_pairs={{0,96},{32,128},{64,160},{96,192},{128,224},{160,256},{192,288},{2... | collective-permute-start | bytes 221192
  440.9 20.0 %collective-permute-start.3 = (bf16[24,3072]{1,0:T(8,128)(2,1)}, bf16[24,3072]{1,0:T(8,128)(2,1)S(1)}, u32[]{:S(2)}, u32[]{:S(2)}) collective-permute-start(bf16[24,3072]{1,0:T(8,128)(2,1)} %get-tuple-element.140), channel_id=1, source_target_pairs={{0,32},{32,64},{64,96},{96,128},{128,160},{160,192},{192,224},{224... | collective-permute-start | bytes 442376
  445.1 15.8 %collective-permute-start.4 = (bf16[24,3072]{1,0:T(8,128)(2,1)}, bf16[24,3072]{1,0:T(8,128)(2,1)S(1)}, u32[]{:S(2)}, u32[]{:S(2)}) collective-permute-start(bf16[24,3072]{1,0:T(8,128)(2,1)} %get-tuple-element.140), channel_id=1, source_target_pairs={{0,64},{32,96},{64,128},{96,160},{128,192},{160,224},{192,256},{22... | collective-permute-start | bytes 442376
  451.5 9.4 %collective-permute-start.5 = (bf16[12,3072]{1,0:T(8,128)(2,1)S(1)}, bf16[12,3072]{1,0:T(8,128)(2,1)S(1)}, u32[]{:S(2)}, u32[]{:S(2)}) collective-permute-start(bf16[12,3072]{1,0:T(8,128)(2,1)S(1)} %slice.1), channel_id=1, source_target_pairs={{0,96},{32,128},{64,160},{96,192},{128,224},{160,256},{192,288},{2... | collective-permute-start | bytes 221192
  463.6 14.6 %all-to-all-start.2 = ((bf16[20,32,96]{2,0,1:T(8,128)(2,1)}), bf16[20,32,96]{2,0,1:T(8,128)(2,1)}, u32[]{:S(2)}, u32[]{:S(2)}) async-start(bf16[20,32,96]{2,0,1:T(8,128)(2,1)} %copy.119), calls=%async_computation.2 | async-start | bytes 393216 | tf_op jit(solution)/shard_map/all_to_all | solution.py:143
  471.7 98.2 %copy-start.8 = (f32[128,2,128]{0,2,1:T(8,128)S(1)}, f32[128,2,128]{0,2,1:T(8,128)}, u32[]{:S(2)}) copy-start(f32[128,2,128]{0,2,1:T(8,128)} %copy-done.7) | copy-start | bytes 393220
  572.4 133.8 %all-reduce.7.cloned.1.call-start = ((), (), s32[]{:S(2)}) async-start(), calls=%async_computation.6 | async-start | bytes 131072 | tf_op jit(solution)/shard_map/psum | solution.py:160
  572.9 202.4 %all-gather.17.cloned.1.call-start = ((), (), s32[]{:S(2)}) async-start(), calls=%async_computation.8 | async-start | bytes 1114112 | tf_op jit(solution)/shard_map/all_gather | solution.py:11
  575.5 12.6 %all-to-all-start = ((bf16[20,32,96]{2,0,1:T(8,128)(2,1)}), bf16[20,32,96]{2,0,1:T(8,128)(2,1)S(1)}, u32[]{:S(2)}, u32[]{:S(2)}) async-start(bf16[20,32,96]{2,0,1:T(8,128)(2,1)} %copy.114), calls=%async_computation | async-start | bytes 393216 | tf_op jit(solution)/shard_map/all_to_all | solution.py:123
  581.6 207.1 %copy-start.21 = (bf16[128,256]{1,0:T(8,128)(2,1)S(1)}, bf16[128,256]{1,0:T(8,128)(2,1)}, u32[]{:S(2)}) copy-start(bf16[128,256]{1,0:T(8,128)(2,1)} %param.20) | copy-start | bytes 196612
  588.2 201.1 %copy-start.23 = (bf16[2,128,128]{2,1,0:T(8,128)(2,1)S(1)}, bf16[2,128,128]{2,1,0:T(8,128)(2,1)}, u32[]{:S(2)}) copy-start(bf16[2,128,128]{2,1,0:T(8,128)(2,1)} %copy-done.22) | copy-start | bytes 196612
  (30 other events, 401.8 us)
Sparse Core Ops, SparseCore 0:
  10.7 75.1 all-gather.14
  87.9 68.8 all-gather.12
  160.5 55.6 all-gather.10
  218.2 73.1 all-gather.20
  293.4 69.9 all-gather.18
  575.2 130.9 all-reduce.6
  708.8 66.4 all-gather.16
where the time goes:
time: 800 us; the launch traced here: 798 us
  waiting for transfers between devices  488 us (61%)
  blocking collectives  178 us (22%)
  starting transfers between devices  47.7 us (6%)
  local copies, waits for them, and re-layouts  29.8 us (4%)
  matrix products  22.5 us (3%)
  other arithmetic  15.8 us (2%)
  between operations  15.6 us (2%)
    all_gather x2, waiting for transfers between devices, carried_in(): gathered = lax.all_gather(value.astype(jnp.bfloat16), axis)  141 us
    psum x1, waiting for transfers between devices, local(): lax.psum(state_part.astype(jnp.bfloat16), 'ctx').astype(jnp.float32)  117 us
    all_gather x1, waiting for transfers between devices, local(): portion = lax.all_gather(expert_in, 'ctx', axis=0, tiled=True)  67.7 us
    psum x1, blocking collectives, local(): inner_sum = lax.psum(jnp.sum(stream_f * scaled_grad, -1), 'ep')  60.3 us
    all_gather x1, waiting for transfers between devices, local(): lax.all_gather(normed_heads, 'ep', axis=1, tiled=True)  59.4 us
    unnamed x1, blocking collectives  52.9 us
    all_gather x1, waiting for transfers between devices, local(): w_cols = lax.all_gather(out_weight, 'ctx', axis=0, tiled=True)  52.8 us
    all_gather x1, waiting for transfers between devices, local(): lax.all_gather(grad_in, 'ctx', axis=0, tiled=True)  38.8 us
  transfers between devices with their start and end apart: 16, of which 9 were waited for; matrix products, arithmetic and copies ran while one was open for 12% of the time, Pallas kernels for 0%

commit v1 on v0

--- a/solution.py
+++ b/solution.py
@@ -2,6 +2,22 @@
 import jax.numpy as jnp
 from jax import lax
 from jax.sharding import PartitionSpec as P
+
+
+def gather_around(x, axis, dim):
+    ways, here, lap = (lax.axis_size(axis), lax.axis_index(axis), x.shape[dim])
+    shape = [n * ways if d == dim else n for d, n in enumerate(x.shape)]
+    full = lax.dynamic_update_slice_in_dim(jnp.zeros(shape, x.dtype), x, here * lap, axis=dim)
+    going_up = going_down = x
+    for far in range(1, ways // 2 + 1):
+        going_up = lax.ppermute(going_up, axis, [(d, (d + 1) % ways) for d in range(ways)])
+        full = lax.dynamic_update_slice_in_dim(full, going_up, (here - far) % ways * lap, axis=dim)
+        if 2 * far < ways:
+            going_down = lax.ppermute(going_down, axis, [(d, (d - 1) % ways) for d in range(ways)])
+            full = lax.dynamic_update_slice_in_dim(
+                full, going_down, (here + far) % ways * lap, axis=dim
+            )
+    return full
 
 
 def carried_in(value, axis, join, neutral, backward):
@@ -80,7 +96,7 @@
         .astype(jnp.bfloat16)
         .reshape(tokens_here, head_count * head_size)
     )
-    w_cols = lax.all_gather(out_weight, "ctx", axis=0, tiled=True)
+    w_cols = gather_around(out_weight, "ctx", 0)
     attn_proj = jnp.dot(
         lax.all_gather(normed_heads, "ep", axis=1, tiled=True), w_cols, preferred_element_type=f32
     )

time: 800 us -> 737 us (0.921)
  waiting for transfers between devices: 488 us -> 360 us
  starting transfers between devices: 47.7 us -> 112 us
    ppermute x0 -> x15, starting transfers between devices: none -> 64.3 us  [the longest x7 46.5 us: gather_around(): lax.ppermute(going_down, axis, [(d, (d - 1) % ways) for d in range(ways)])]
    all_gather x1, waiting for transfers between devices: 59.4 us -> 0.02 us  [local(): lax.all_gather(normed_heads, 'ep', axis=1, tiled=True)]
    all_gather x1 -> x0, waiting for transfers between devices: 52.8 us -> none  [local(): w_cols = lax.all_gather(out_weight, 'ctx', axis=0, tiled=True)]
    all_gather x1, waiting for transfers between devices: 38.8 us -> 11.2 us  [local(): lax.all_gather(grad_in, 'ctx', axis=0, tiled=True)]
    ppermute x0 -> x15, waiting for transfers between devices: none -> 12.2 us  [the longest x8 12.2 us: gather_around(): lax.ppermute(going_up, axis, [(d, (d + 1) % ways) for d in range(ways)])]
    unnamed x89 -> x87, local copies, waits for them, and re-layouts: 19.3 us -> 19.3 us
  transfers between devices with their start and end apart: 16 -> 30, of which waited for: 9 -> 15; matrix products, arithmetic and copies ran while one was open for 12% -> 13% of each run, Pallas kernels for 0% -> 0%
where the time goes in v1:
time: 737 us; the launch traced here: 735 us
  waiting for transfers between devices  360 us (49%)
  blocking collectives  178 us (24%)
  starting transfers between devices  112 us (15%)
  local copies, waits for them, and re-layouts  30.4 us (4%)
  matrix products  22 us (3%)
  between operations  16.2 us (2%)
  other arithmetic  15.8 us (2%)
    all_gather x2, waiting for transfers between devices, carried_in(): gathered = lax.all_gather(value.astype(jnp.bfloat16), axis)  141 us
    psum x1, waiting for transfers between devices, local(): lax.psum(state_part.astype(jnp.bfloat16), 'ctx').astype(jnp.float32)  117 us
    all_gather x1, waiting for transfers between devices, local(): portion = lax.all_gather(expert_in, 'ctx', axis=0, tiled=True)  67.6 us
    psum x1, blocking collectives, local(): inner_sum = lax.psum(jnp.sum(stream_f * scaled_grad, -1), 'ep')  60.3 us
    unnamed x1, blocking collectives  52.9 us
    ppermute x7, starting transfers between devices, gather_around(): lax.ppermute(going_down, axis, [(d, (d - 1) % ways) for d in range(ways)])  46.5 us
    unnamed x6, starting transfers between devices  28.1 us
    all_gather x1, blocking collectives, local(): lax.all_gather(grad_stream, 'ep', axis=1, tiled=True)  27.4 us
  transfers between devices with their start and end apart: 30, of which 15 were waited for; matrix products, arithmetic and copies ran while one was open for 13% of the time, Pallas kernels for 0%

profile of v1, /device:TPU:2, one launch (start us, length us, event | category | flops | bytes accessed | tf_op | source)
XLA Modules:
  0.0 734.5 jit_solution(17222544006566006718)
XLA Ops:
  12.1 73.7 %all-gather.12.cloned.1.call-done = bf16[32,128,128]{2,1,0:T(8,128)(2,1)} async-done(((bf16[2,128,128]{2,1,0:T(8,128)(2,1)}), bf16[32,128,128]{2,1,0:T(8,128)(2,1)}) %all-gather.12.cloned.1.call-update) | async-done | bytes 1048592 | tf_op jit(solution)/shard_map/all_gather | solution.py:27
  88.5 14.3 %all_to_all.67 = bf16[32,20,96]{2,1,0:T(8,128)(2,1)S(1)} all-to-all(bf16[32,20,96]{2,1,0:T(8,128)(2,1)S(1)} %all_to_all.53), channel_id=1, replica_groups=mesh['ctx'=16,'ep'=32] {'ep'}, dimensions={0} | all-to-all | bytes 245760 | tf_op jit(solution)/shard_map/all_to_all | solution.py:144
  108.2 15.6 %collective-permute-start.1 = (bf16[512,96]{0,1:T(8,128)(2,1)S(1)}, bf16[512,96]{0,1:T(8,128)(2,1)S(1)}, u32[]{:S(2)}, u32[]{:S(2)}) collective-permute-start(bf16[512,96]{0,1:T(8,128)(2,1)S(1)} %copy-done.25), channel_id=1, source_target_pairs={{0,480},{32,0},{64,32},{96,64},{128,96},{160,128},{192,160},{224,1... | collective-permute-start | bytes 294920 | tf_op jit(solution)/shard_map/ppermute | solution.py:16
  127.1 5.1 collective-permute-start.3
  134.8 5.1 collective-permute-start.5
  142.5 5.1 collective-permute-start.7
  165.7 5.2 collective-permute-start.13
  174.4 7.1 collective-permute-done.14
  184.3 22.8 %all_gather.30 = bf16[128,3072]{0,1:T(8,128)(2,1)S(1)} all-gather(bf16[128,96]{0,1:T(8,128)(2,1)S(1)} %fusion.33), channel_id=1, replica_groups=mesh['ctx'=16,'ep'=32] {'ep'}, dimensions={1}, use_global_device_ids=true | all-gather | bytes 811008 | tf_op jit(solution)/shard_map/all_gather | solution.py:116
  210.8 6.0 all-to-all-start.3
  216.8 11.2 %all-gather.18.cloned.1.call-done = bf16[16,20,3072]{2,1,0:T(8,128)(2,1)} async-done(((bf16[1,20,3072]{2,1,0:T(8,128)(2,1)}), bf16[16,20,3072]{2,1,0:T(8,128)(2,1)}) %all-gather.18.cloned.1.call-update) | async-done | bytes 1966096 | tf_op jit(solution)/shard_map/all_gather | solution.py:145
  232.3 67.6 %all-gather.16.cloned.1.call-done = bf16[16,20,3072]{2,1,0:T(8,128)(2,1)} async-done(((bf16[1,20,3072]{2,1,0:T(8,128)(2,1)}), bf16[16,20,3072]{2,1,0:T(8,128)(2,1)}) %all-gather.16.cloned.1.call-update) | async-done | bytes 1966096 | tf_op jit(solution)/shard_map/all_gather | solution.py:127
  310.0 52.9 %fusion.70 = (bf16[24,3072]{1,0:T(8,128)(2,1)}, bf16[24,3072]{1,0:T(8,128)(2,1)}) fusion(bf16[320,3072]{1,0:T(8,128)(2,1)S(1)} %convolution_convert_fusion, bf16[320,3072]{1,0:T(8,128)(2,1)} %fusion.2), kind=kCustom, calls=%all-reduce-scatter.2 | all-reduce-scatter fusion | flops 2359297 | bytes 4229120
  363.9 5.3 collective-permute-start.15
  369.1 6.7 collective-permute-start.16
  381.7 5.4 collective-permute-start.19
  400.1 7.5 %all-to-all-start.2 = ((bf16[20,32,96]{2,0,1:T(8,128)(2,1)}), bf16[20,32,96]{2,0,1:T(8,128)(2,1)}, u32[]{:S(2)}, u32[]{:S(2)}) async-start(bf16[20,32,96]{2,0,1:T(8,128)(2,1)} %copy.118), calls=%async_computation.2 | async-start | bytes 393216 | tf_op jit(solution)/shard_map/all_to_all | solution.py:159
  417.2 60.3 %psum.14 = f32[128]{0:T(128)S(1)} all-reduce(f32[128]{0:T(128)} %get-tuple-element.145), channel_id=1, replica_groups=mesh['ctx'=16,'ep'=32] {'ep'}, use_global_device_ids=true, to_apply=%region_9.10 | all-reduce | flops 128 | bytes 1024 | tf_op jit(solution)/shard_map/psum | solution.py:162
  478.9 27.4 %all_gather.33 = bf16[128,3072]{0,1:T(8,128)(2,1)S(1)} all-gather(bf16[128,96]{0,1:T(8,128)(2,1)S(1)} %fusion.59), channel_id=1, replica_groups=mesh['ctx'=16,'ep'=32] {'ep'}, dimensions={1}, use_global_device_ids=true | all-gather | bytes 811008 | tf_op jit(solution)/shard_map/all_gather | solution.py:169
  511.9 5.6 all-to-all-start
  518.8 5.7 all-to-all-done
  525.5 117.4 %all-reduce.7.cloned.1.call-done = bf16[2,128,128]{1,2,0:T(8,128)(2,1)} async-done(((bf16[2,128,128]{1,2,0:T(8,128)(2,1)}), bf16[2,128,128]{1,2,0:T(8,128)(2,1)}) %all-reduce.7.cloned.1.call-update) | async-done | bytes 65552 | tf_op jit(solution)/shard_map/psum | solution.py:176
  644.5 67.4 %all-gather.14.cloned.1.call-done = bf16[32,128,128]{2,1,0:T(8,128)(2,1)} async-done(((bf16[2,128,128]{2,1,0:T(8,128)(2,1)}), bf16[32,128,128]{2,1,0:T(8,128)(2,1)}) %all-gather.14.cloned.1.call-update) | async-done | bytes 1048592 | tf_op jit(solution)/shard_map/all_gather | solution.py:27
  711.9 13.4 %while.23 = (s32[]{:T(128)}, f32[2,128,128]{2,1,0:T(8,128)S(1)}, s32[]{:T(128)}, bf16[16,2,128,128]{3,2,1,0:T(8,128)(2,1)}, s32[]{:T(128)}, /*index=5*/s32[]{:T(128)}, s32[]{:T(128)}, s32[]{:T(128)}) while((s32[]{:T(128)}, f32[2,128,128]{2,1,0:T(8,128)S(1)}, s32[]{:T(128)}, bf16[16,2,128,128]{3,2,1,0:T(8,128)(2,1)}, s32[]{:T(128)}, ...), condition=%wide.region_12.13_spmd, body=%wide.region_11.12_spmd.sunk | while | flops 65542 | bytes 327815 | solution.py:34
  (224 shorter events, 117.4 us)
Async XLA Ops:
  7.2 78.6 %all-gather.12.cloned.1.call-start = ((), (), s32[]{:S(2)}) async-start(), calls=%async_computation.6 | async-start | bytes 1114112 | tf_op jit(solution)/shard_map/all_gather | solution.py:27
  10.0 171.6 %all-gather.10.cloned.1.call-start = ((), (), s32[]{:S(2)}) async-start(), calls=%async_computation.4 | async-start | bytes 2162688 | tf_op jit(solution)/shard_map/all_gather | solution.py:101
  87.3 140.7 %all-gather.18.cloned.1.call-start = ((), (), s32[]{:S(2)}) async-start(), calls=%async_computation.9 | async-start | bytes 2506752 | tf_op jit(solution)/shard_map/all_gather | solution.py:145
  103.7 196.2 %all-gather.16.cloned.1.call-start = ((), (), s32[]{:S(2)}) async-start(), calls=%async_computation.8 | async-start | bytes 2506752 | tf_op jit(solution)/shard_map/all_gather | solution.py:127
  103.8 21.4 %collective-permute-start = (bf16[512,96]{0,1:T(8,128)(2,1)S(1)}, bf16[512,96]{0,1:T(8,128)(2,1)S(1)}, u32[]{:S(2)}, u32[]{:S(2)}) collective-permute-start(bf16[512,96]{0,1:T(8,128)(2,1)S(1)} %copy-done.25), channel_id=1, source_target_pairs={{0,32},{32,64},{64,96},{96,128},{128,160},{160,192},{192,224},{224... | collective-permute-start | bytes 294920 | tf_op jit(solution)/shard_map/ppermute | solution.py:13
  108.2 18.9 %collective-permute-start.1 = (bf16[512,96]{0,1:T(8,128)(2,1)S(1)}, bf16[512,96]{0,1:T(8,128)(2,1)S(1)}, u32[]{:S(2)}, u32[]{:S(2)}) collective-permute-start(bf16[512,96]{0,1:T(8,128)(2,1)S(1)} %copy-done.25), channel_id=1, source_target_pairs={{0,480},{32,0},{64,32},{96,64},{128,96},{160,128},{192,160},{224,1... | collective-permute-start | bytes 294920 | tf_op jit(solution)/shard_map/ppermute | solution.py:16
  125.2 7.7 %collective-permute-start.2 = (bf16[512,96]{0,1:T(8,128)(2,1)S(1)}, bf16[512,96]{0,1:T(8,128)(2,1)S(1)}, u32[]{:S(2)}, u32[]{:S(2)}) collective-permute-start(bf16[512,96]{0,1:T(8,128)(2,1)S(1)} %collective-permute-done), channel_id=1, source_target_pairs={{0,32},{32,64},{64,96},{96,128},{128,160},{160,192},{192,224},{224... | collective-permute-start | bytes 294920 | tf_op jit(solution)/shard_map/ppermute | solution.py:13
  132.9 7.7 %collective-permute-start.4 = (bf16[512,96]{0,1:T(8,128)(2,1)S(1)}, bf16[512,96]{0,1:T(8,128)(2,1)S(1)}, u32[]{:S(2)}, u32[]{:S(2)}) collective-permute-start(bf16[512,96]{0,1:T(8,128)(2,1)S(1)} %collective-permute-done.2), channel_id=1, source_target_pairs={{0,32},{32,64},{64,96},{96,128},{128,160},{160,192},{192,224},{224... | collective-permute-start | bytes 294920 | tf_op jit(solution)/shard_map/ppermute | solution.py:13
  140.6 7.7 %collective-permute-start.6 = (bf16[512,96]{0,1:T(8,128)(2,1)S(1)}, bf16[512,96]{0,1:T(8,128)(2,1)S(1)}, u32[]{:S(2)}, u32[]{:S(2)}) collective-permute-start(bf16[512,96]{0,1:T(8,128)(2,1)S(1)} %collective-permute-done.4), channel_id=1, source_target_pairs={{0,32},{32,64},{64,96},{96,128},{128,160},{160,192},{192,224},{224... | collective-permute-start | bytes 294920 | tf_op jit(solution)/shard_map/ppermute | solution.py:13
  148.3 7.7 %collective-permute-start.8 = (bf16[512,96]{0,1:T(8,128)(2,1)S(1)}, bf16[512,96]{0,1:T(8,128)(2,1)S(1)}, u32[]{:S(2)}, u32[]{:S(2)}) collective-permute-start(bf16[512,96]{0,1:T(8,128)(2,1)S(1)} %collective-permute-done.6), channel_id=1, source_target_pairs={{0,32},{32,64},{64,96},{96,128},{128,160},{160,192},{192,224},{224... | collective-permute-start | bytes 294920 | tf_op jit(solution)/shard_map/ppermute | solution.py:13
  163.7 8.7 %collective-permute-start.12 = (bf16[512,96]{0,1:T(8,128)(2,1)S(1)}, bf16[512,96]{0,1:T(8,128)(2,1)S(1)}, u32[]{:S(2)}, u32[]{:S(2)}) collective-permute-start(bf16[512,96]{0,1:T(8,128)(2,1)S(1)} %collective-permute-done.10), channel_id=1, source_target_pairs={{0,32},{32,64},{64,96},{96,128},{128,160},{160,192},{192,224},{224... | collective-permute-start | bytes 294920 | tf_op jit(solution)/shard_map/ppermute | solution.py:13
  165.7 8.7 %collective-permute-start.13 = (bf16[512,96]{0,1:T(8,128)(2,1)S(1)}, bf16[512,96]{0,1:T(8,128)(2,1)S(1)}, u32[]{:S(2)}, u32[]{:S(2)}) collective-permute-start(bf16[512,96]{0,1:T(8,128)(2,1)S(1)} %collective-permute-done.11), channel_id=1, source_target_pairs={{0,480},{32,0},{64,32},{96,64},{128,96},{160,128},{192,160},{224,1... | collective-permute-start | bytes 294920 | tf_op jit(solution)/shard_map/ppermute | solution.py:16
  172.4 9.1 %collective-permute-start.14 = (bf16[512,96]{0,1:T(8,128)(2,1)S(1)}, bf16[512,96]{0,1:T(8,128)(2,1)S(1)}, u32[]{:S(2)}, u32[]{:S(2)}) collective-permute-start(bf16[512,96]{0,1:T(8,128)(2,1)S(1)} %collective-permute-done.12), channel_id=1, source_target_pairs={{0,32},{32,64},{64,96},{96,128},{128,160},{160,192},{192,224},{224... | collective-permute-start | bytes 294920 | tf_op jit(solution)/shard_map/ppermute | solution.py:13
  210.8 189.3 %all-to-all-start.3 = ((bf16[32,256,96]{1,2,0:T(8,128)(2,1)}), bf16[32,256,96]{1,2,0:T(8,128)(2,1)}, u32[]{:S(2)}, u32[]{:S(2)}) async-start(bf16[32,256,96]{1,2,0:T(8,128)(2,1)} %bitcast.161), calls=%async_computation.3 | async-start | bytes 3145728 | tf_op jit(solution)/shard_map/all_to_all | solution.py:168
  363.9 31.0 %collective-permute-start.15 = (bf16[24,3072]{1,0:T(8,128)(2,1)}, bf16[24,3072]{1,0:T(8,128)(2,1)S(1)}, u32[]{:S(2)}, u32[]{:S(2)}) collective-permute-start(bf16[24,3072]{1,0:T(8,128)(2,1)} %get-tuple-element.139), channel_id=1, source_target_pairs={{0,32},{32,64},{64,96},{96,128},{128,160},{160,192},{192,224},{224... | collective-permute-start | bytes 442376
  369.1 25.7 %collective-permute-start.16 = (bf16[24,3072]{1,0:T(8,128)(2,1)}, bf16[24,3072]{1,0:T(8,128)(2,1)S(1)}, u32[]{:S(2)}, u32[]{:S(2)}) collective-permute-start(bf16[24,3072]{1,0:T(8,128)(2,1)} %get-tuple-element.139), channel_id=1, source_target_pairs={{0,64},{32,96},{64,128},{96,160},{128,192},{160,224},{192,256},{22... | collective-permute-start | bytes 442376
  375.9 12.2 %collective-permute-start.17 = (bf16[12,3072]{1,0:T(8,128)(2,1)S(1)}, bf16[12,3072]{1,0:T(8,128)(2,1)S(1)}, u32[]{:S(2)}, u32[]{:S(2)}) collective-permute-start(bf16[12,3072]{1,0:T(8,128)(2,1)S(1)} %slice), channel_id=1, source_target_pairs={{0,96},{32,128},{64,160},{96,192},{128,224},{160,256},{192,288},{2... | collective-permute-start | bytes 221192
  377.5 19.8 %collective-permute-start.18 = (bf16[24,3072]{1,0:T(8,128)(2,1)}, bf16[24,3072]{1,0:T(8,128)(2,1)S(1)}, u32[]{:S(2)}, u32[]{:S(2)}) collective-permute-start(bf16[24,3072]{1,0:T(8,128)(2,1)} %get-tuple-element.140), channel_id=1, source_target_pairs={{0,32},{32,64},{64,96},{96,128},{128,160},{160,192},{192,224},{224... | collective-permute-start | bytes 442376
  381.7 15.6 %collective-permute-start.19 = (bf16[24,3072]{1,0:T(8,128)(2,1)}, bf16[24,3072]{1,0:T(8,128)(2,1)S(1)}, u32[]{:S(2)}, u32[]{:S(2)}) collective-permute-start(bf16[24,3072]{1,0:T(8,128)(2,1)} %get-tuple-element.140), channel_id=1, source_target_pairs={{0,64},{32,96},{64,128},{96,160},{128,192},{160,224},{192,256},{22... | collective-permute-start | bytes 442376
  388.1 9.3 %collective-permute-start.20 = (bf16[12,3072]{1,0:T(8,128)(2,1)S(1)}, bf16[12,3072]{1,0:T(8,128)(2,1)S(1)}, u32[]{:S(2)}, u32[]{:S(2)}) collective-permute-start(bf16[12,3072]{1,0:T(8,128)(2,1)S(1)} %slice.1), channel_id=1, source_target_pairs={{0,96},{32,128},{64,160},{96,192},{128,224},{160,256},{192,288},{2... | collective-permute-start | bytes 221192
  400.1 14.6 %all-to-all-start.2 = ((bf16[20,32,96]{2,0,1:T(8,128)(2,1)}), bf16[20,32,96]{2,0,1:T(8,128)(2,1)}, u32[]{:S(2)}, u32[]{:S(2)}) async-start(bf16[20,32,96]{2,0,1:T(8,128)(2,1)} %copy.118), calls=%async_computation.2 | async-start | bytes 393216 | tf_op jit(solution)/shard_map/all_to_all | solution.py:159
  508.8 134.0 %all-reduce.7.cloned.1.call-start = ((), (), s32[]{:S(2)}) async-start(), calls=%async_computation.5 | async-start | bytes 131072 | tf_op jit(solution)/shard_map/psum | solution.py:176
  509.4 202.5 %all-gather.14.cloned.1.call-start = ((), (), s32[]{:S(2)}) async-start(), calls=%async_computation.7 | async-start | bytes 1114112 | tf_op jit(solution)/shard_map/all_gather | solution.py:27
  511.9 12.6 %all-to-all-start = ((bf16[20,32,96]{2,0,1:T(8,128)(2,1)}), bf16[20,32,96]{2,0,1:T(8,128)(2,1)S(1)}, u32[]{:S(2)}, u32[]{:S(2)}) async-start(bf16[20,32,96]{2,0,1:T(8,128)(2,1)} %copy.113), calls=%async_computation | async-start | bytes 393216 | tf_op jit(solution)/shard_map/all_to_all | solution.py:139
  (43 other events, 1422.4 us)
Sparse Core Ops, SparseCore 0:
  10.7 75.1 all-gather.11
  89.5 63.0 all-gather.9
  154.7 73.2 all-gather.17
  230.0 69.8 all-gather.15
  511.7 131.1 all-reduce.6
  645.4 66.4 all-gather.13
